TPU v7x, 256 devices: a whole 4x4x8 slice. The times are simulated.
256 devices in a mesh: batch: 16 (over z, core), wx: 4 (over y), wy: 4 (over x).
Axes of the slice: x: 4, y: 4, z: 8, core: 2. Of those that a mesh axis runs over, the one named last changes fastest.
Arguments:
- tokens: bfloat16 [8192, 16384], P(('batch', 'wx'), 'wy'), may hold values from -6 to 6
- routes: int32 [8192, 1], P(('batch', 'wx')), may hold values from 0 to 15; in each aligned block of 128 rows (0 to 127, 128 to 255, ...) at most 16 rows name the same one
- gate_weight: bfloat16 [16384, 2048], P('wy', 'wx'), may hold values from -0.046875 to 0.046875
- up_weight: bfloat16 [16384, 2048], P('wy', 'wx'), may hold values from -0.046875 to 0.046875
Outputs:
- hidden: bfloat16 [16384, 2048], P(('batch', 'wy'), 'wx')
Inputs may be any that keep to these rules, and one draw needn't show every extreme that they name: `routes`: among the tokens of one device, at most 16 share a group.
All inputs are finite; a program needn't handle non-finite values.
Results may differ from a plain program's by a relative error of at most 0.001.
Values may be sent and summed in bfloat16 or wider, within the bound.
No kernel may reach another device: no remote copies, remote signals or barrier semaphores. Data moves between devices by JAX's collectives and lax.ppermute only.
A program may use at most 128 MiB of HBM per device.

v0:
```python
import jax
import jax.numpy as jnp
from jax import lax
from jax.sharding import PartitionSpec as P


def place_rows(source, group_of, slots, groups_total):
    onehot = (group_of[:, None] == jnp.arange(groups_total, dtype=jnp.int32)[None, :]).astype(
        jnp.int32
    )
    ordinal = jnp.sum((jnp.cumsum(onehot, axis=0) - onehot) * onehot, axis=1)
    target = group_of * slots + ordinal
    chooser = (
        target[:, None] == jnp.arange(groups_total * slots, dtype=jnp.int32)[None, :]
    ).astype(jnp.bfloat16)
    placed = lax.dot_general(
        chooser, source, (((0,), (0,)), ((), ())), preferred_element_type=jnp.float32
    )
    return placed.astype(jnp.bfloat16)


def per_device(tokens, routes, gate_weight, up_weight):
    row_count = tokens.shape[0]
    hid = gate_weight.shape[1]
    groups_total = lax.axis_size("batch")
    wx_count = lax.axis_size("wx")
    slots = 2 * row_count // groups_total
    gathered = lax.all_gather(tokens, "wx", axis=0, tiled=True)
    group_all = lax.all_gather(routes, "wx", axis=0, tiled=True)
    gate = jnp.dot(gathered, gate_weight, preferred_element_type=jnp.float32)
    up = jnp.dot(gathered, up_weight, preferred_element_type=jnp.float32)
    both = jnp.concatenate([gate, up], axis=1)
    summed = lax.psum_scatter(both, "wy", scatter_dimension=0, tiled=True)
    gate_sum, up_sum = (summed[:, :hid], summed[:, hid:])
    hidden = (jax.nn.silu(gate_sum) * up_sum).astype(jnp.bfloat16)
    own = lax.axis_index("wy")
    group_of = lax.dynamic_slice_in_dim(group_all.reshape(wx_count, row_count), own, 1, 0)[0]
    placed = place_rows(hidden, group_of, slots, groups_total)
    placed = placed.reshape(groups_total, slots, hid)
    arrived = lax.all_to_all(placed, "batch", split_axis=0, concat_axis=0, tiled=True)
    return arrived.reshape(groups_total * slots, hid)


def solution(mesh):
    placed = (P(("batch", "wx"), "wy"), P(("batch", "wx"), None), P("wy", "wx"), P("wy", "wx"))
    return jax.shard_map(
        per_device, mesh=mesh, in_specs=placed, out_specs=P(("batch", "wy"), "wx"), check_vma=False
    )
```

profile of v0, /device:TPU:1, one launch (start us, length us, event | category | flops | bytes accessed | tf_op | source)
XLA Modules:
  0.0 134.4 jit_solution(3706500899102372639)
XLA Ops:
  6.5 0.0 all-gather.2.cloned.1.call-start
  6.5 0.7 all-gather.2.cloned.1.call-update
  7.3 0.0 reduce-scatter.2.cloned.1.call-start
  7.3 56.3 %all-gather.2.cloned.1.call-done = bf16[512,4096]{1,0:T(8,128)(2,1)} async-done(((bf16[128,4096]{1,0:T(8,128)(2,1)}), bf16[512,4096]{1,0:T(8,128)(2,1)}) %all-gather.2.cloned.1.call-update) | async-done | bytes 4194320 | tf_op jit(solution)/shard_map/all_gather | solution.py:28
  63.6 0.0 copy-start.1
  63.6 0.0 copy-start.2
  63.6 6.0 %fusion.8 = f32[512,512]{0,1:T(8,128)S(1)} fusion(bf16[512,4096]{1,0:T(8,128)(2,1)} %all-gather.2.cloned.1.call-done, bf16[4096,512]{1,0:T(8,128)(2,1)} %param.7), kind=kOutput, calls=%fused_computation.14 | convolution fusion | flops 2147483648 | bytes 9437184 | tf_op jit(solution)/shard_map/dot_general | solution.py:31
  69.6 0.0 copy-done.1
  69.6 0.0 copy-done.2
  69.6 2.4 %fusion.7 = f32[512,512]{0,1:T(8,128)S(1)} fusion(bf16[512,4096]{1,0:T(8,128)(2,1)S(1)} %copy-done.2, bf16[4096,512]{1,0:T(8,128)(2,1)S(1)} %copy-done.1), kind=kOutput, calls=%fused_computation.13 | convolution fusion | flops 2147483648 | bytes 9437184 | tf_op jit(solution)/shard_map/dot_general | solution.py:30
  72.0 0.0 copy-start
  72.0 1.5 %pad_maximum_fusion = f32[512,1024]{0,1:T(8,128)} fusion(f32[512,512]{0,1:T(8,128)S(1)} %fusion.8, f32[512,512]{0,1:T(8,128)S(1)} %fusion.7), kind=kLoop, calls=%fused_computation | loop fusion | flops 524288 | bytes 4194304 | tf_op jit(solution)/shard_map/concatenate | solution.py:32
  73.5 0.0 reduce-scatter.2.cloned.1.call-update
  73.5 0.0 copy-done
  73.5 5.8 %all_gather.6 = s32[512,1]{0,1:T(1,128)S(1)} all-gather(s32[128,1]{0,1:T(1,128)S(1)} %copy-done), channel_id=1, replica_groups=mesh['batch'=16,'wx'=4,'wy'=4] {'wx'}, dimensions={0}, use_global_device_ids=true | all-gather | bytes 2560 | tf_op jit(solution)/shard_map/all_gather | solution.py:29
  79.3 0.1 fusion.5
  79.4 0.2 reduce_window_sum.11
  79.6 0.2 select_reduce_fusion
  79.8 26.6 %reduce-scatter.2.cloned.1.call-done = f32[128,1024]{0,1:T(8,128)} async-done(((f32[512,1024]{0,1:T(8,128)}), f32[128,1024]{0,1:T(8,128)}) %reduce-scatter.2.cloned.1.call-update) | async-done | bytes 524304 | tf_op jit(solution)/shard_map/reduce_scatter | solution.py:33
  106.3 1.3 %convolution_convert_fusion = bf16[256,512]{1,0:T(8,128)(2,1)S(1)} fusion(f32[128,1024]{0,1:T(8,128)} %reduce-scatter.2.cloned.1.call-done, s32[128]{0:T(128)S(1)} %multiply_add_fusion), kind=kOutput, calls=%fused_computation.1 | convolution fusion | flops 34144256 | bytes 786944 | tf_op jit(solution)/shard_map/dot_general | solution.py:16
  107.7 19.1 %all_to_all.5 = bf16[16,16,512]{2,1,0:T(8,128)(2,1)S(1)} all-to-all(bf16[16,16,512]{2,1,0:T(8,128)(2,1)S(1)} %bitcast.12), channel_id=1, replica_groups=mesh['batch'=16,'wx'=4,'wy'=4] {'batch'}, dimensions={0} | all-to-all | bytes 524288 | tf_op jit(solution)/shard_map/all_to_all | solution.py:40
  126.8 0.7 copy.6
  (2 shorter events, 0.0 us)
Async XLA Ops:
  6.5 57.0 %all-gather.2.cloned.1.call-start = ((), (), s32[]{:S(2)}) async-start(), calls=%async_computation.2 | async-start | bytes 5242880 | tf_op jit(solution)/shard_map/all_gather | solution.py:28
  7.3 99.1 %reduce-scatter.2.cloned.1.call-start = ((), (), s32[]{:S(2)}) async-start(), calls=%async_computation.3 | async-start | bytes 2621440 | tf_op jit(solution)/shard_map/reduce_scatter | solution.py:33
  63.6 6.0 %copy-start.1 = (bf16[4096,512]{1,0:T(8,128)(2,1)S(1)}, bf16[4096,512]{1,0:T(8,128)(2,1)}, u32[]{:S(2)}) copy-start(bf16[4096,512]{1,0:T(8,128)(2,1)} %param.6) | copy-start | bytes 12582916
  63.6 6.0 %copy-start.2 = (bf16[512,4096]{1,0:T(8,128)(2,1)S(1)}, bf16[512,4096]{1,0:T(8,128)(2,1)}, u32[]{:S(2)}) copy-start(bf16[512,4096]{1,0:T(8,128)(2,1)} %all-gather.2.cloned.1.call-done) | copy-start | bytes 12582916
  72.0 1.6 %copy-start = (s32[128,1]{0,1:T(1,128)S(1)}, s32[128,1]{0,1:T(1,128)}, u32[]{:S(2)}) copy-start(s32[128,1]{0,1:T(1,128)} %param.5) | copy-start | bytes 1540
Sparse Core Ops, SparseCore 0:
  9.1 54.3 all-gather.1
  73.6 32.6 reduce-scatter.1
where the time goes:
time: 135 us; the launch traced here: 134 us
  waiting for transfers between devices  83.6 us (62%)
  blocking collectives  24.9 us (18%)
  between operations  13.5 us (10%)
  matrix products  9.68 us (7%)
  other arithmetic  1.96 us (1%)
    all_gather x1, waiting for transfers between devices, per_device(): gathered = lax.all_gather(tokens, 'wx', axis=0, tiled=True)  56.3 us
    reduce_scatter x1, waiting for transfers between devices, per_device(): summed = lax.psum_scatter(both, 'wy', scatter_dimension=0, tiled=True)  26.6 us
    all_to_all x1, blocking collectives, per_device(): lax.all_to_all(placed, 'batch', split_axis=0, concat_axis=0, tiled=True)  19.1 us
    dot_general x1, matrix products, per_device(): up = jnp.dot(gathered, up_weight, preferred_element_type=jnp.float32)  5.97 us
    all_gather x1, blocking collectives, per_device(): group_all = lax.all_gather(routes, 'wx', axis=0, tiled=True)  5.78 us
  transfers between devices with their start and end apart: 2, of which 2 were waited for; matrix products, arithmetic and copies ran while one was open for 0% of the time, Pallas kernels for 0%

commit v1 on v0

--- a/solution.py
+++ b/solution.py
@@ -25,7 +25,9 @@
     groups_total = lax.axis_size("batch")
     wx_count = lax.axis_size("wx")
     slots = 2 * row_count // groups_total
-    gathered = lax.all_gather(tokens, "wx", axis=0, tiled=True)
+    gathered = jnp.concatenate(
+        lax.all_to_all(jnp.stack([tokens] * lax.axis_size("wx")), "wx", 0, 0), axis=0
+    )
     group_all = lax.all_gather(routes, "wx", axis=0, tiled=True)
     gate = jnp.dot(gathered, gate_weight, preferred_element_type=jnp.float32)
     up = jnp.dot(gathered, up_weight, preferred_element_type=jnp.float32)

time: 135 us -> 130 us (0.963)
  waiting for transfers between devices: 83.6 us -> 27.8 us
  blocking collectives: 24.9 us -> 78.3 us
  matrix products: 9.68 us -> 6.08 us
  local copies, waits for them, and re-layouts: 0.72 us -> 2.44 us
    all_gather x1 -> x0, waiting for transfers between devices: 56.3 us -> none  [per_device(): gathered = lax.all_gather(tokens, 'wx', axis=0, tiled=True)]
    all_to_all x0 -> x1, blocking collectives: none -> 53 us  [per_device(): lax.all_to_all(jnp.stack([tokens] * lax.axis_size('wx')), 'wx', 0, 0)]
    dot_general x1, matrix products: 5.97 us -> 2.37 us  [per_device(): up = jnp.dot(gathered, up_weight, preferred_element_type=jnp.float32)]
    another operation x0 -> x1, local copies, waits for them, and re-layouts: none -> 1.72 us  [per_device(): jnp.stack([tokens] * lax.axis_size('wx'))]
  transfers between devices with their start and end apart: 2 -> 1, of which waited for: 2 -> 1; matrix products, arithmetic and copies ran while one was open for 0% -> 0% of each run, Pallas kernels for 0% -> 0%
where the time goes in v1:
time: 130 us
  blocking collectives  78.3 us (60%)
  waiting for transfers between devices  27.8 us (21%)
  between operations  13.5 us (10%)
  matrix products  6.08 us (5%)
  local copies, waits for them, and re-layouts  2.44 us (2%)
  other arithmetic  1.96 us (2%)
    all_to_all x1, blocking collectives, per_device(): lax.all_to_all(jnp.stack([tokens] * lax.axis_size('wx')), 'wx', 0, 0)  53 us
    reduce_scatter x1, waiting for transfers between devices, per_device(): summed = lax.psum_scatter(both, 'wy', scatter_dimension=0, tiled=True)  27.8 us
    all_to_all x1, blocking collectives, per_device(): lax.all_to_all(placed, 'batch', split_axis=0, concat_axis=0, tiled=True)  19.1 us
    all_gather x1, blocking collectives, per_device(): group_all = lax.all_gather(routes, 'wx', axis=0, tiled=True)  6.11 us
  transfers between devices with their start and end apart: 1, of which 1 were waited for; matrix products, arithmetic and copies ran while one was open for 0% of the time, Pallas kernels for 0%

profile of v1, /device:TPU:1, one launch (start us, length us, event | category | flops | bytes accessed | tf_op | source)
XLA Modules:
  0.0 130.1 jit_solution(16882946619607163542)
XLA Ops:
  6.5 0.0 reduce-scatter.2.cloned.1.call-start
  6.5 1.7 %stack.2 = bf16[4,128,4096]{2,1,0:T(8,128)(2,1)S(1)} broadcast(bf16[128,4096]{1,0:T(8,128)(2,1)} %param.4), dimensions={1,2} | broadcast | bytes 5242880 | tf_op jit(solution)/shard_map/stack | solution.py:29
  8.3 0.0 copy-start.1
  8.3 53.0 %all_to_all.10 = bf16[4,128,4096]{2,1,0:T(8,128)(2,1)S(1)} all-to-all(bf16[4,128,4096]{2,1,0:T(8,128)(2,1)S(1)} %stack.2), channel_id=1, replica_groups=mesh['batch'=16,'wx'=4,'wy'=4] {'wx'}, dimensions={0} | all-to-all | bytes 8388608 | tf_op jit(solution)/shard_map/all_to_all | solution.py:29
  61.3 0.0 copy-done.1
  61.3 0.0 copy-start.2
  61.3 2.4 %fusion.8 = f32[512,512]{0,1:T(8,128)S(1)} fusion(bf16[512,4096]{1,0:T(8,128)(2,1)S(1)} %bitcast.12, bf16[4096,512]{1,0:T(8,128)(2,1)S(1)} %copy-done.1), kind=kOutput, calls=%fused_computation.14 | convolution fusion | flops 2147483648 | bytes 9437184 | tf_op jit(solution)/shard_map/dot_general | solution.py:33
  63.7 0.0 copy-done.2
  63.7 2.4 %fusion.7 = f32[512,512]{0,1:T(8,128)S(1)} fusion(bf16[512,4096]{1,0:T(8,128)(2,1)S(1)} %bitcast.13, bf16[4096,512]{1,0:T(8,128)(2,1)S(1)} %copy-done.2), kind=kOutput, calls=%fused_computation.13 | convolution fusion | flops 2147483648 | bytes 9437184 | tf_op jit(solution)/shard_map/dot_general | solution.py:32
  66.0 0.0 copy-start
  66.1 1.5 %pad_maximum_fusion = f32[512,1024]{0,1:T(8,128)} fusion(f32[512,512]{0,1:T(8,128)S(1)} %fusion.8, f32[512,512]{0,1:T(8,128)S(1)} %fusion.7), kind=kLoop, calls=%fused_computation | loop fusion | flops 524288 | bytes 4194304 | tf_op jit(solution)/shard_map/concatenate | solution.py:34
  67.6 0.0 reduce-scatter.2.cloned.1.call-update
  67.6 0.0 copy-done
  67.6 6.1 %all_gather.3 = s32[512,1]{0,1:T(1,128)S(1)} all-gather(s32[128,1]{0,1:T(1,128)S(1)} %copy-done), channel_id=1, replica_groups=mesh['batch'=16,'wx'=4,'wy'=4] {'wx'}, dimensions={0}, use_global_device_ids=true | all-gather | bytes 2560 | tf_op jit(solution)/shard_map/all_gather | solution.py:31
  73.7 0.1 fusion.5
  73.8 0.2 reduce_window_sum.11
  74.0 0.2 select_reduce_fusion
  74.2 27.8 %reduce-scatter.2.cloned.1.call-done = f32[128,1024]{0,1:T(8,128)} async-done(((f32[512,1024]{0,1:T(8,128)}), f32[128,1024]{0,1:T(8,128)}) %reduce-scatter.2.cloned.1.call-update) | async-done | bytes 524304 | tf_op jit(solution)/shard_map/reduce_scatter | solution.py:35
  102.0 1.3 %convolution_convert_fusion = bf16[256,512]{1,0:T(8,128)(2,1)S(1)} fusion(f32[128,1024]{0,1:T(8,128)} %reduce-scatter.2.cloned.1.call-done, s32[128]{0:T(128)S(1)} %multiply_add_fusion), kind=kOutput, calls=%fused_computation.1 | convolution fusion | flops 34144256 | bytes 786944 | tf_op jit(solution)/shard_map/dot_general | solution.py:16
  103.4 19.1 %all_to_all.11 = bf16[16,16,512]{2,1,0:T(8,128)(2,1)S(1)} all-to-all(bf16[16,16,512]{2,1,0:T(8,128)(2,1)S(1)} %bitcast.15), channel_id=1, replica_groups=mesh['batch'=16,'wx'=4,'wy'=4] {'batch'}, dimensions={0} | all-to-all | bytes 524288 | tf_op jit(solution)/shard_map/all_to_all | solution.py:42
  122.5 0.7 copy.6
  (2 shorter events, 0.0 us)
Async XLA Ops:
  6.5 95.5 %reduce-scatter.2.cloned.1.call-start = ((), (), s32[]{:S(2)}) async-start(), calls=%async_computation.3 | async-start | bytes 2621440 | tf_op jit(solution)/shard_map/reduce_scatter | solution.py:35
  8.3 53.0 %copy-start.1 = (bf16[4096,512]{1,0:T(8,128)(2,1)S(1)}, bf16[4096,512]{1,0:T(8,128)(2,1)}, u32[]{:S(2)}) copy-start(bf16[4096,512]{1,0:T(8,128)(2,1)} %param.7) | copy-start | bytes 12582916
  61.3 2.4 %copy-start.2 = (bf16[4096,512]{1,0:T(8,128)(2,1)S(1)}, bf16[4096,512]{1,0:T(8,128)(2,1)}, u32[]{:S(2)}) copy-start(bf16[4096,512]{1,0:T(8,128)(2,1)} %param.6) | copy-start | bytes 12582916
  66.0 1.6 %copy-start = (s32[128,1]{0,1:T(1,128)S(1)}, s32[128,1]{0,1:T(1,128)}, u32[]{:S(2)}) copy-start(s32[128,1]{0,1:T(1,128)} %param.5) | copy-start | bytes 1540
Sparse Core Ops, SparseCore 0:
  67.7 34.2 reduce-scatter.1
